TPU v7x, 256 devices: a whole 4x4x8 slice. The times are simulated.
256 devices in a mesh: seq: 16 (over x, y), exp: 16 (over z, core).
Axes of the slice: x: 4, y: 4, z: 8, core: 2. Of those that a mesh axis runs over, the one named last changes fastest.
Arguments:
- mixer_input: bfloat16 [16384, 4096], P('seq', 'exp'), may hold values from -6 to 6
- gate_input: bfloat16 [16384, 4096], P('seq', 'exp'), may hold values from -6 to 6
- write_keys: bfloat16 [16384, 128], P('seq'), may hold values from -6 to 6
- read_queries: bfloat16 [16384, 128], P('seq'), may hold values from -0.5 to 0.5
- step_size: float32 [64, 16384], P('exp', 'seq'), may hold values from 0 to 1, as said below
- log_decay: float32 [64, 16384], P('exp', 'seq'), may hold values from -1 to 0, as said below
- skip_gain: float32 [64], P('exp'), may hold values from 0.5 to 1.5
- out_weight: bfloat16 [4096, 2048], P('exp'), may hold values from -0.09375 to 0.09375
- residual: bfloat16 [16384, 2048], P(('seq', 'exp')), may hold values from -6 to 6
- norm_gain: float32 [2048], replicated, may hold values from 0.25 to 1.75
- routes: int32 [16384, 6], P(('seq', 'exp')), may hold values from 0 to 63, all different within a row; in each aligned block of 64 rows (0 to 63, 64 to 127, ...) at most 8 rows name the same one
- route_weight: float32 [16384, 6], P(('seq', 'exp')), may hold values from 0.1 to 0.5
- expert_gate: bfloat16 [256, 352, 2048], P(('seq', 'exp')), may hold values from -0.125 to 0.125
- expert_up: bfloat16 [256, 352, 2048], P(('seq', 'exp')), may hold values from -0.125 to 0.125
- expert_down: bfloat16 [256, 352, 2048], P(('seq', 'exp')), may hold values from -0.15625 to 0.15625
Outputs:
- block_output: bfloat16 [16384, 2048], P(('seq', 'exp'))
Inputs may be any that keep to these rules, and one draw needn't show every extreme that they name: `routes`: each row names 6 different experts; in each aligned block of 64 rows (the rows of one device) no expert is named by more than 8 rows, a bound that some block reaches. `step_size`: positive. `log_decay`: not positive.
All inputs are finite; a program needn't handle non-finite values.
Results may differ from a plain program's by a relative error of at most 0.015.
Values may be sent and summed in bfloat16 or wider, within the bound.
No kernel may reach another device: no remote copies, remote signals or barrier semaphores. Data moves between devices by JAX's collectives and lax.ppermute only.
A program may use at most 128 MiB of HBM per device.

v0:
```python
import jax
import jax.numpy as jnp
from jax import lax
from jax.sharding import PartitionSpec as P

HEAD_DIM = 64
STATE = 128
TOP = 6
SPLIT = 4
STRETCH = 256


def prefix(shard, axis, join, neutral):
    place = lax.axis_index(axis)
    gathered = jax.tree.map(
        lambda a, kind: lax.all_gather(a.astype(kind), axis), shard, (jnp.bfloat16, jnp.bfloat16)
    )
    state = jax.tree.map(lambda a, e: jnp.zeros_like(a) + jnp.asarray(e, a.dtype), shard, neutral)

    def one(turn, state):
        return join(
            state,
            jax.tree.map(
                lambda a, own: lax.dynamic_index_in_dim(a, turn, 0, False).astype(own.dtype),
                gathered,
                shard,
            ),
        )

    return lax.fori_loop(0, place, one, state)


def join_states(earlier, later_part):
    return (
        earlier[0] + later_part[0],
        jnp.exp(later_part[0])[:, None, None] * earlier[1] + later_part[1],
    )


def shards(
    mixer_input,
    gate_input,
    write_keys,
    read_queries,
    step_size,
    log_decay,
    skip_gain,
    out_weight,
    residual,
    norm_gain,
    routes,
    route_weight,
    expert_gate,
    expert_up,
    expert_down,
):
    length = mixer_input.shape[0]
    head_count = step_size.shape[0]
    blocks = length // STRETCH
    inputs = mixer_input.reshape(blocks, STRETCH, head_count, HEAD_DIM)
    key_rows = write_keys.reshape(blocks, STRETCH, STATE)
    queries = read_queries.reshape(blocks, STRETCH, STATE)
    step_rows = step_size.reshape(head_count, blocks, STRETCH).transpose(1, 0, 2)
    cumulative = jnp.cumsum(log_decay.reshape(head_count, blocks, STRETCH), axis=2).transpose(
        1, 0, 2
    )
    location_values = jnp.arange(STRETCH, dtype=jnp.int32)
    causal = location_values[:, None] >= location_values[None, :]
    scores = jnp.einsum("cin,cjn->cij", queries, key_rows, preferred_element_type=jnp.float32)
    spread = cumulative[:, :, :, None] - cumulative[:, :, None, :]
    decays = jnp.where(causal, jnp.exp(jnp.where(causal, spread, 0.0)), 0.0)
    mixing = (scores[:, None] * decays * step_rows[:, :, None, :]).astype(jnp.bfloat16)
    local_out = jnp.einsum("chij,cjhp->cihp", mixing, inputs, preferred_element_type=jnp.float32)
    tail_scale = jnp.exp(cumulative[:, :, -1:] - cumulative) * step_rows
    weighted = (inputs.astype(jnp.float32) * tail_scale.transpose(0, 2, 1)[..., None]).astype(
        jnp.bfloat16
    )
    block_state = jnp.einsum(
        "cjhp,cjn->chpn", weighted, key_rows, preferred_element_type=jnp.float32
    )
    totals = cumulative[:, :, -1]

    def advance(carry_state, pieces):
        block_total, fresh_state = pieces
        return (jnp.exp(block_total)[:, None, None] * carry_state + fresh_state, carry_state)

    zero_state = jnp.zeros((head_count, HEAD_DIM, STATE), jnp.float32)
    end_local, entering_local = lax.scan(advance, zero_state, (totals, block_state))
    device_decay = jnp.sum(totals, axis=0)
    before = prefix(
        (device_decay, end_local), "seq", join_states, (jnp.zeros_like(device_decay), zero_state)
    )
    before_state = before[1]
    before_blocks = jnp.cumsum(totals, axis=0) - totals
    entering = jnp.exp(before_blocks)[:, :, None, None] * before_state[None] + entering_local
    carried = jnp.einsum(
        "cin,chpn->cihp", queries.astype(jnp.float32), entering, precision=lax.Precision.HIGHEST
    )
    carried = carried * jnp.exp(cumulative).transpose(0, 2, 1)[..., None]
    result = local_out + carried + skip_gain[None, None, :, None] * inputs.astype(jnp.float32)
    gated_out = (
        result.reshape(length, head_count * HEAD_DIM) * jax.nn.silu(gate_input.astype(jnp.float32))
    ).astype(jnp.bfloat16)
    row_count = residual.shape[0]
    mixer_out = lax.psum_scatter(
        jnp.dot(gated_out, out_weight, preferred_element_type=jnp.float32).astype(jnp.bfloat16),
        "exp",
        scatter_dimension=0,
        tiled=True,
    ).astype(jnp.float32)
    stream = (residual.astype(jnp.float32) + mixer_out).astype(jnp.bfloat16)
    widened = stream.astype(jnp.float32)
    normed = (
        widened * lax.rsqrt(jnp.mean(widened * widened, axis=-1, keepdims=True) + 1e-06) * norm_gain
    ).astype(jnp.bfloat16)
    seq_count = lax.axis_size("seq")
    exp_count = lax.axis_size("exp")
    row_experts = exp_count // SPLIT
    experts = seq_count * row_experts
    capacity = min(row_count, max(2, (4 * TOP * row_count + 3 * experts - 1) // (3 * experts)))
    flat_routes = routes.reshape(-1)
    onehot = (flat_routes[:, None] == jnp.arange(experts, dtype=jnp.int32)[None, :]).astype(
        jnp.int32
    )
    earlier_count = jnp.cumsum(onehot, axis=0) - onehot
    slot_index = jnp.sum(earlier_count * onehot, axis=1)
    target = (
        flat_routes % row_experts * (seq_count * capacity)
        + flat_routes // row_experts * capacity
        + slot_index
    )
    owner_row = jnp.arange(flat_routes.shape[0], dtype=jnp.int32) // TOP
    source = jnp.zeros((experts * capacity,), jnp.int32).at[target].set(owner_row)
    filled = jnp.zeros((experts * capacity,), jnp.bool_).at[target].set(True)
    outgoing = jnp.where(filled[:, None], normed[source], jnp.zeros((), jnp.bfloat16))
    outgoing = outgoing.reshape(row_experts, seq_count, capacity, -1)
    arrived = lax.all_to_all(outgoing, "seq", split_axis=1, concat_axis=1, tiled=True)
    copies = jnp.repeat(arrived, SPLIT, axis=0)
    block = lax.all_to_all(copies, "exp", split_axis=0, concat_axis=0, tiled=True)
    flat_rows = block.reshape(-1, block.shape[-1])
    contract = (((1,), (1,)), ((), ()))
    gate_val = lax.dot_general(
        flat_rows, expert_gate[0], contract, preferred_element_type=jnp.float32
    )
    up_val = lax.dot_general(flat_rows, expert_up[0], contract, preferred_element_type=jnp.float32)
    activated = (jax.nn.silu(gate_val) * up_val).astype(jnp.bfloat16)
    piece_out = jnp.dot(activated, expert_down[0], preferred_element_type=jnp.float32).astype(
        jnp.bfloat16
    )
    piece_out = piece_out.reshape(block.shape)
    returned = lax.all_to_all(
        lax.all_to_all(piece_out, "seq", split_axis=1, concat_axis=1, tiled=True),
        "exp",
        split_axis=0,
        concat_axis=0,
        tiled=True,
    )
    summed = jnp.sum(
        returned.reshape(row_experts, SPLIT, seq_count, capacity, -1).astype(jnp.float32), axis=1
    )
    results = summed.reshape(experts * capacity, -1)[target]
    expert_sum = jnp.sum(
        (results * route_weight.reshape(-1)[:, None]).reshape(row_count, TOP, -1), axis=1
    )
    return (stream.astype(jnp.float32) + expert_sum).astype(jnp.bfloat16)


def solution(mesh):
    return jax.shard_map(
        shards,
        mesh=mesh,
        in_specs=(
            P("seq", "exp"),
            P("seq", "exp"),
            P("seq", None),
            P("seq", None),
            P("exp", "seq"),
            P("exp", "seq"),
            P("exp"),
            P("exp", None),
            P(("seq", "exp"), None),
            P(),
            P(("seq", "exp"), None),
            P(("seq", "exp"), None),
            P(("seq", "exp"), None, None),
            P(("seq", "exp"), None, None),
            P(("seq", "exp"), None, None),
        ),
        out_specs=P(("seq", "exp"), None),
        check_vma=False,
    )
```

profile of v0, /device:TPU:1, one launch (start us, length us, event | category | flops | bytes accessed | tf_op | source)
XLA Modules:
  0.0 738.1 jit_solution(7842727586102235308)
XLA Ops:
  7.4 4.8 reduce-window.14
  13.8 2.0 reshape.309
  16.5 1.3 fusion.29
  17.8 3.1 while.26
  23.2 34.3 %all-reduce = bf16[64]{0:T(256)(128)(2,1)S(1)} all-reduce(bf16[64]{0:T(256)(128)(2,1)S(1)} %dynamic-update-slice), channel_id=2, replica_groups=mesh['seq'=16,'exp'=16] {'seq'}, use_global_device_ids=true, to_apply=%add | all-reduce | flops 64 | bytes 256
  57.6 2.1 copy.77
  60.7 1.4 fusion.14
  62.1 9.7 %all-gather.4.cloned.1.call-done = bf16[64,64,128]{2,1,0:T(8,128)(2,1)} async-done(((bf16[4,64,128]{2,1,0:T(8,128)(2,1)}), bf16[64,64,128]{2,1,0:T(8,128)(2,1)}) %all-gather.4.cloned.1.call-update) | async-done | bytes 1048592 | tf_op jit(solution)/shard_map/all_gather | solution.py:16
  71.9 1.9 fusion.17
  74.7 3.3 convolution_convert_fusion.1
  80.6 2.9 scatter_custom_fusion.1
  83.5 2.1 scatter_custom_fusion
  85.8 66.6 %reduce-scatter.2.cloned.1.call-done = bf16[64,2048]{1,0:T(8,128)(2,1)} async-done(((bf16[1024,2048]{1,0:T(8,128)(2,1)}), bf16[64,2048]{1,0:T(8,128)(2,1)}) %reduce-scatter.2.cloned.1.call-update) | async-done | bytes 262160 | tf_op jit(solution)/shard_map/reduce_scatter | solution.py:105
  152.5 1.1 fusion.24
  153.6 1.1 fusion.26
  154.7 3.3 gather_fusion
  158.0 1.8 copy_select_fusion
  159.8 29.3 %all_to_all.20 = bf16[4,16,8,2048]{3,2,0,1:T(8,128)(2,1)S(1)} all-to-all(bf16[4,16,8,2048]{3,2,0,1:T(8,128)(2,1)S(1)} %copy_select_fusion), channel_id=1, replica_groups=mesh['seq'=16,'exp'=16] {'seq'}, dimensions={1} | all-to-all | bytes 4194304 | tf_op jit(solution)/shard_map/all_to_all | solution.py:137
  189.4 1.1 broadcast_in_dim.79
  190.5 198.7 %all_to_all.21 = bf16[16,16,8,2048]{3,2,1,0:T(8,128)(2,1)S(1)} all-to-all(bf16[16,16,8,2048]{3,2,1,0:T(8,128)(2,1)S(1)} %bitcast.116), channel_id=1, replica_groups=mesh['seq'=16,'exp'=16] {'exp'}, dimensions={0} | all-to-all | bytes 16777216 | tf_op jit(solution)/shard_map/all_to_all | solution.py:139
  389.2 3.2 fusion.12
  392.5 3.5 fusion.2
  396.0 6.8 convolution_convert_fusion
  402.8 8.3 %copy.85 = bf16[16,16,8,2048]{3,2,0,1:T(8,128)(2,1)} copy(bf16[16,16,8,2048]{3,2,1,0:T(8,128)(2,1)} %bitcast.120) | data formatting | bytes 16777216 | tf_op jit(solution)/shard_map/reshape | solution.py:150
  411.1 100.0 %all_to_all.22 = bf16[16,16,8,2048]{3,2,0,1:T(8,128)(2,1)} all-to-all(bf16[16,16,8,2048]{3,2,0,1:T(8,128)(2,1)} %copy.85), channel_id=1, replica_groups=mesh['seq'=16,'exp'=16] {'seq'}, dimensions={1} | all-to-all | bytes 16777216 | tf_op jit(solution)/shard_map/all_to_all | solution.py:152
  511.1 8.3 %copy.86 = bf16[16,16,8,2048]{3,2,1,0:T(8,128)(2,1)} copy(bf16[16,16,8,2048]{3,2,0,1:T(8,128)(2,1)} %all_to_all.22) | data formatting | bytes 16777216 | tf_op jit(solution)/shard_map/all_to_all | solution.py:152
  519.4 4.8 all-to-all-start.3
  524.3 182.6 %all-to-all-done.3 = bf16[16,16,8,2048]{3,2,1,0:T(8,128)(2,1)} async-done(((bf16[16,16,8,2048]{3,2,1,0:T(8,128)(2,1)}), bf16[16,16,8,2048]{3,2,1,0:T(8,128)(2,1)}, u32[]{:S(2)}, u32[]{:S(2)}) %all-to-all-start.3) | async-done | bytes 8388640 | tf_op jit(solution)/shard_map/all_to_all | solution.py:151
  706.9 7.8 %convert_reduce_fusion = f32[4,16,8,2048]{3,2,1,0:T(8,128)} fusion(bf16[16,16,8,2048]{3,2,1,0:T(8,128)(2,1)} %all-to-all-done.3), kind=kLoop, calls=%fused_computation.11 | loop fusion | flops 7340032 | bytes 12582912 | tf_op jit(solution)/shard_map/reduce_sum | solution.py:158
  714.7 7.3 gather_fusion.1
  722.0 4.7 gather.13
  726.7 3.8 multiply_reduce_fusion
  (101 shorter events, 13.4 us)
Async XLA Ops:
  6.5 389.5 %copy-start = (bf16[1,352,2048]{2,1,0:T(8,128)(2,1)S(1)}, bf16[1,352,2048]{2,1,0:T(8,128)(2,1)}, u32[]{:S(2)}) copy-start(bf16[1,352,2048]{2,1,0:T(8,128)(2,1)} %param.33) | copy-start | bytes 4325380
  6.5 9.8 %copy-start.8 = (f32[4,1024]{1,0:T(4,128)S(1)}, f32[4,1024]{1,0:T(4,128)}, u32[]{:S(2)}) copy-start(f32[4,1024]{1,0:T(4,128)} %param.23) | copy-start | bytes 49156
  6.5 65.3 %all-gather.4.cloned.1.call-start = ((), (), s32[]{:S(2)}) async-start(), calls=%async_computation.6 | async-start | bytes 1114112 | tf_op jit(solution)/shard_map/all_gather | solution.py:16
  13.0 0.8 copy-start.6
  15.8 5.9 copy-start.16
  16.5 43.9 %copy-start.4 = (bf16[1024,128]{1,0:T(8,128)(2,1)S(1)}, bf16[1024,128]{1,0:T(8,128)(2,1)}, u32[]{:S(2)}) copy-start(bf16[1024,128]{1,0:T(8,128)(2,1)} %param.22) | copy-start | bytes 786436
  16.5 43.9 %copy-start.5 = (bf16[1024,128]{1,0:T(8,128)(2,1)S(1)}, bf16[1024,128]{1,0:T(8,128)(2,1)}, u32[]{:S(2)}) copy-start(bf16[1024,128]{1,0:T(8,128)(2,1)} %param.21) | copy-start | bytes 786436
  21.6 130.9 %reduce-scatter.2.cloned.1.call-start = ((), (), s32[]{:S(2)}) async-start(), calls=%async_computation.5 | async-start | bytes 4456448 | tf_op jit(solution)/shard_map/reduce_scatter | solution.py:105
  60.7 11.2 %copy-start.12 = (f32[4]{0:T(128)S(1)}, f32[4]{0:T(128)}, u32[]{:S(2)}) copy-start(f32[4]{0:T(128)} %param.25) | copy-start | bytes 52
  71.9 2.8 copy-start.7
  71.9 2.8 copy-start.15
  78.0 0.7 copy-start.10
  78.0 74.4 %copy-start.2 = (bf16[64,2048]{1,0:T(8,128)(2,1)S(1)}, bf16[64,2048]{1,0:T(8,128)(2,1)}, u32[]{:S(2)}) copy-start(bf16[64,2048]{1,0:T(8,128)(2,1)} %param.27) | copy-start | bytes 786436
  78.0 75.6 %copy-start.9 = (f32[2048]{0:T(1024)S(1)}, f32[2048]{0:T(1024)}, u32[]{:S(2)}) copy-start(f32[2048]{0:T(1024)} %param.28) | copy-start | bytes 24580
  190.5 198.7 %copy-start.13 = (bf16[1,352,2048]{2,1,0:T(8,128)(2,1)S(1)}, bf16[1,352,2048]{2,1,0:T(8,128)(2,1)}, u32[]{:S(2)}) copy-start(bf16[1,352,2048]{2,1,0:T(8,128)(2,1)} %param.31) | copy-start | bytes 4325380
  389.2 3.2 copy-start.14
  519.4 4.8 copy-start.11
  519.4 187.5 %all-to-all-start.3 = ((bf16[16,16,8,2048]{3,2,1,0:T(8,128)(2,1)}), bf16[16,16,8,2048]{3,2,1,0:T(8,128)(2,1)}, u32[]{:S(2)}, u32[]{:S(2)}) async-start(bf16[16,16,8,2048]{3,2,1,0:T(8,128)(2,1)} %copy.86), calls=%async_computation.4 | async-start | bytes 16777216 | tf_op jit(solution)/shard_map/all_to_all | solution.py:151
  722.0 9.3 %copy-start.1 = (bf16[1,352,2048]{2,1,0:T(8,128)(2,1)S(1)}, bf16[1,352,2048]{2,1,0:T(8,128)(2,1)}, u32[]{:S(2)}) copy-start(bf16[1,352,2048]{2,1,0:T(8,128)(2,1)} %param.33) | copy-start | bytes 4325380
  726.7 3.8 copy-start.3
Sparse Core Ops, SparseCore 0:
  21.7 50.0 all-gather.3
  78.2 74.2 reduce-scatter.1
where the time goes:
time: 740 us; the launch traced here: 738 us
  blocking collectives  362 us (49%)
  waiting for transfers between devices  259 us (35%)
  local copies, waits for them, and re-layouts  48.7 us (7%)
  other arithmetic  26.9 us (4%)
  matrix products  21.7 us (3%)
  between operations  14.5 us (2%)
    all_to_all x1, blocking collectives, shards(): lax.all_to_all(copies, 'exp', split_axis=0, concat_axis=0, tiled=True)  199 us
    all_to_all x1, waiting for transfers between devices, shards(): lax.all_to_all(lax.all_to_all(piece_out, 'seq', split_axis=1, concat_axis...  183 us
    all_to_all x1, blocking collectives, shards(): lax.all_to_all(piece_out, 'seq', split_axis=1, concat_axis=1, tiled=True)  100 us
    reduce_scatter x1, waiting for transfers between devices, shards(): lax.psum_scatter(jnp.dot(gated_out, out_weight, preferred_element_type=jn...  66.6 us
    unnamed x1, blocking collectives  34.3 us
    all_to_all x1, blocking collectives, shards(): lax.all_to_all(outgoing, 'seq', split_axis=1, concat_axis=1, tiled=True)  29.3 us
  transfers between devices with their start and end apart: 3, of which 3 were waited for; matrix products, arithmetic and copies ran while one was open for 2% of the time, Pallas kernels for 0%

commit v1 on v0

--- a/solution.py
+++ b/solution.py
@@ -8,6 +8,13 @@
 TOP = 6
 SPLIT = 4
 STRETCH = 256
+
+
+def swap_blocks(array, name, split, join):
+    size = lax.axis_size(name)
+    pieces = jnp.stack(jnp.split(array, size, axis=split), axis=0)
+    pieces = lax.all_to_all(pieces, name, split_axis=0, concat_axis=0)
+    return jnp.concatenate(pieces, axis=join)
 
 
 def prefix(shard, axis, join, neutral):
@@ -149,11 +156,7 @@
     )
     piece_out = piece_out.reshape(block.shape)
     returned = lax.all_to_all(
-        lax.all_to_all(piece_out, "seq", split_axis=1, concat_axis=1, tiled=True),
-        "exp",
-        split_axis=0,
-        concat_axis=0,
-        tiled=True,
+        swap_blocks(piece_out, "seq", 1, 1), "exp", split_axis=0, concat_axis=0, tiled=True
     )
     summed = jnp.sum(
         returned.reshape(row_experts, SPLIT, seq_count, capacity, -1).astype(jnp.float32), axis=1

time: 740 us -> 731 us (0.988)
  local copies, waits for them, and re-layouts: 48.7 us -> 40.3 us
    all_to_all x1 -> x0, local copies, waits for them, and re-layouts: 8.26 us -> none  [shards(): lax.all_to_all(piece_out, 'seq', split_axis=1, concat_axis=1, tiled=True)]
where the time goes in v1:
time: 731 us; the launch traced here: 729 us
  blocking collectives  361 us (49%)
  waiting for transfers between devices  259 us (35%)
  local copies, waits for them, and re-layouts  40.3 us (6%)
  other arithmetic  27.6 us (4%)
  matrix products  22 us (3%)
  between operations  14.6 us (2%)
    all_to_all x1, blocking collectives, shards(): lax.all_to_all(copies, 'exp', split_axis=0, concat_axis=0, tiled=True)  199 us
    all_to_all x1, waiting for transfers between devices, shards(): lax.all_to_all(swap_blocks(piece_out, 'seq', 1, 1), 'exp', split_axis=0,...  183 us
    all_to_all x1, blocking collectives, swap_blocks(): pieces = lax.all_to_all(pieces, name, split_axis=0, concat_axis=0)  98.7 us
    reduce_scatter x1, waiting for transfers between devices, shards(): lax.psum_scatter(jnp.dot(gated_out, out_weight, preferred_element_type=jn...  67.3 us
    unnamed x1, blocking collectives  34.3 us
    all_to_all x1, blocking collectives, shards(): lax.all_to_all(outgoing, 'seq', split_axis=1, concat_axis=1, tiled=True)  29.3 us
  transfers between devices with their start and end apart: 3, of which 3 were waited for; matrix products, arithmetic and copies ran while one was open for 2% of the time, Pallas kernels for 0%

profile of v1, /device:TPU:1, one launch (start us, length us, event | category | flops | bytes accessed | tf_op | source)
XLA Modules:
  0.0 729.3 jit_solution(2057017843514948010)
XLA Ops:
  7.5 4.8 reduce-window.14
  13.8 2.0 reshape.317
  17.2 1.2 fusion.29
  18.5 3.1 while.26
  23.9 34.3 %all-reduce = bf16[64]{0:T(256)(128)(2,1)S(1)} all-reduce(bf16[64]{0:T(256)(128)(2,1)S(1)} %dynamic-update-slice), channel_id=2, replica_groups=mesh['seq'=16,'exp'=16] {'seq'}, use_global_device_ids=true, to_apply=%add | all-reduce | flops 64 | bytes 256
  58.3 2.0 copy.124
  61.0 1.2 fusion.74
  62.3 1.4 fusion.14
  63.7 8.8 %all-gather.4.cloned.1.call-done = bf16[64,64,128]{2,1,0:T(8,128)(2,1)} async-done(((bf16[4,64,128]{2,1,0:T(8,128)(2,1)}), bf16[64,64,128]{2,1,0:T(8,128)(2,1)}) %all-gather.4.cloned.1.call-update) | async-done | bytes 1048592 | tf_op jit(solution)/shard_map/all_gather | solution.py:23
  72.6 1.8 fusion.17
  75.3 4.7 convolution_convert_fusion.1
  81.9 2.9 scatter_custom_fusion.1
  84.8 2.1 scatter_custom_fusion
  87.1 67.3 %reduce-scatter.2.cloned.1.call-done = bf16[64,2048]{1,0:T(8,128)(2,1)} async-done(((bf16[1024,2048]{1,0:T(8,128)(2,1)}), bf16[64,2048]{1,0:T(8,128)(2,1)}) %reduce-scatter.2.cloned.1.call-update) | async-done | bytes 262160 | tf_op jit(solution)/shard_map/reduce_scatter | solution.py:112
  154.5 1.1 fusion.24
  155.6 1.1 fusion.26
  156.7 3.3 gather_fusion
  160.0 1.8 copy_select_fusion
  161.8 29.3 %all_to_all.20 = bf16[4,16,8,2048]{3,2,0,1:T(8,128)(2,1)S(1)} all-to-all(bf16[4,16,8,2048]{3,2,0,1:T(8,128)(2,1)S(1)} %copy_select_fusion), channel_id=1, replica_groups=mesh['seq'=16,'exp'=16] {'seq'}, dimensions={1} | all-to-all | bytes 4194304 | tf_op jit(solution)/shard_map/all_to_all | solution.py:144
  191.4 1.1 broadcast_in_dim.79
  192.5 198.7 %all_to_all.21 = bf16[16,16,8,2048]{3,2,1,0:T(8,128)(2,1)S(1)} all-to-all(bf16[16,16,8,2048]{3,2,1,0:T(8,128)(2,1)S(1)} %bitcast.215), channel_id=1, replica_groups=mesh['seq'=16,'exp'=16] {'exp'}, dimensions={0} | all-to-all | bytes 16777216 | tf_op jit(solution)/shard_map/all_to_all | solution.py:146
  391.2 3.2 fusion.12
  394.5 3.6 fusion.2
  398.1 4.8 convolution_convert_fusion
  403.6 98.7 %all_to_all.22 = bf16[16,16,1,8,2048]{4,3,1,2,0:T(8,128)(2,1)} all-to-all(bf16[16,16,1,8,2048]{4,3,1,2,0:T(8,128)(2,1)S(1)} %fusion.31), channel_id=1, replica_groups=mesh['seq'=16,'exp'=16] {'seq'}, dimensions={0} | all-to-all | bytes 16777216 | tf_op jit(solution)/shard_map/all_to_all | solution.py:16
  502.3 8.3 %copy.148 = bf16[16,16,8,2048]{3,2,1,0:T(8,128)(2,1)} copy(bf16[16,16,8,2048]{3,2,0,1:T(8,128)(2,1)} %bitcast.216) | data formatting | bytes 16777216 | tf_op jit(solution)/shard_map/reshape | solution.py:17
  510.6 4.8 all-to-all-start.3
  515.5 182.6 %all-to-all-done.3 = bf16[16,16,8,2048]{3,2,1,0:T(8,128)(2,1)} async-done(((bf16[16,16,8,2048]{3,2,1,0:T(8,128)(2,1)}), bf16[16,16,8,2048]{3,2,1,0:T(8,128)(2,1)}, u32[]{:S(2)}, u32[]{:S(2)}) %all-to-all-start.3) | async-done | bytes 8388640 | tf_op jit(solution)/shard_map/all_to_all | solution.py:158
  698.1 7.8 %convert_reduce_fusion = f32[4,16,8,2048]{3,2,1,0:T(8,128)} fusion(bf16[16,16,8,2048]{3,2,1,0:T(8,128)(2,1)} %all-to-all-done.3), kind=kLoop, calls=%fused_computation.11 | loop fusion | flops 7340032 | bytes 12582912 | tf_op jit(solution)/shard_map/reduce_sum | solution.py:161
  705.9 7.4 %gather_fusion.1 = f32[384,2048]{1,0:T(8,128)} fusion(f32[512,2048]{1,0:T(8,128)} %bitcast.214, s32[1024]{0:T(1024)S(1)} %pad_clamp_fusion), kind=kCustom, calls=%fused_computation.1 | custom fusion | bytes 6292992 | tf_op jit(solution)/shard_map/gather | solution.py:164
  713.3 4.6 gather.13
  717.9 3.7 multiply_reduce_fusion
  (110 shorter events, 13.8 us)
Async XLA Ops:
  6.5 391.5 %copy-start = (bf16[1,352,2048]{2,1,0:T(8,128)(2,1)S(1)}, bf16[1,352,2048]{2,1,0:T(8,128)(2,1)}, u32[]{:S(2)}) copy-start(bf16[1,352,2048]{2,1,0:T(8,128)(2,1)} %param.33) | copy-start | bytes 4325380
  6.5 15.9 %copy-start.13 = (u32[256]{0:T(256)S(1)}, u32[256]{0:T(256)}, u32[]{:S(2)}) copy-start(u32[256]{0:T(256)} %constant.118) | copy-start | bytes 3076
  6.5 15.8 %copy-start.6 = (f32[4,1024]{1,0:T(4,128)S(1)}, f32[4,1024]{1,0:T(4,128)}, u32[]{:S(2)}) copy-start(f32[4,1024]{1,0:T(4,128)} %param.23) | copy-start | bytes 49156
  6.5 54.5 %copy-start.4 = (bf16[1024,128]{1,0:T(8,128)(2,1)S(1)}, bf16[1024,128]{1,0:T(8,128)(2,1)}, u32[]{:S(2)}) copy-start(bf16[1024,128]{1,0:T(8,128)(2,1)} %param.22) | copy-start | bytes 786436
  6.5 66.0 %all-gather.4.cloned.1.call-start = ((), (), s32[]{:S(2)}) async-start(), calls=%async_computation.6 | async-start | bytes 1114112 | tf_op jit(solution)/shard_map/all_gather | solution.py:23
  13.0 0.8 copy-start.5
  18.5 54.1 %copy-start.10 = (f32[4]{0:T(128)S(1)}, f32[4]{0:T(128)}, u32[]{:S(2)}) copy-start(f32[4]{0:T(128)} %param.25) | copy-start | bytes 52
  22.3 132.2 %reduce-scatter.2.cloned.1.call-start = ((), (), s32[]{:S(2)}) async-start(), calls=%async_computation.5 | async-start | bytes 4456448 | tf_op jit(solution)/shard_map/reduce_scatter | solution.py:112
  75.2 4.8 copy-start.8
  75.3 79.2 %copy-start.2 = (bf16[64,2048]{1,0:T(8,128)(2,1)S(1)}, bf16[64,2048]{1,0:T(8,128)(2,1)}, u32[]{:S(2)}) copy-start(bf16[64,2048]{1,0:T(8,128)(2,1)} %param.27) | copy-start | bytes 786436
  75.3 80.3 %copy-start.7 = (f32[2048]{0:T(1024)S(1)}, f32[2048]{0:T(1024)}, u32[]{:S(2)}) copy-start(f32[2048]{0:T(1024)} %param.28) | copy-start | bytes 24580
  192.5 198.7 %copy-start.11 = (bf16[1,352,2048]{2,1,0:T(8,128)(2,1)S(1)}, bf16[1,352,2048]{2,1,0:T(8,128)(2,1)}, u32[]{:S(2)}) copy-start(bf16[1,352,2048]{2,1,0:T(8,128)(2,1)} %param.31) | copy-start | bytes 4325380
  391.2 3.2 copy-start.12
  510.6 4.8 copy-start.9
  510.6 187.5 %all-to-all-start.3 = ((bf16[16,16,8,2048]{3,2,1,0:T(8,128)(2,1)}), bf16[16,16,8,2048]{3,2,1,0:T(8,128)(2,1)}, u32[]{:S(2)}, u32[]{:S(2)}) async-start(bf16[16,16,8,2048]{3,2,1,0:T(8,128)(2,1)} %copy.148), calls=%async_computation.4 | async-start | bytes 16777216 | tf_op jit(solution)/shard_map/all_to_all | solution.py:158
  705.9 16.6 %copy-start.1 = (bf16[1,352,2048]{2,1,0:T(8,128)(2,1)S(1)}, bf16[1,352,2048]{2,1,0:T(8,128)(2,1)}, u32[]{:S(2)}) copy-start(bf16[1,352,2048]{2,1,0:T(8,128)(2,1)} %param.33) | copy-start | bytes 4325380
  713.3 8.4 %copy-start.3 = (bf16[64,2048]{1,0:T(8,128)(2,1)S(1)}, bf16[64,2048]{1,0:T(8,128)(2,1)}, u32[]{:S(2)}) copy-start(bf16[64,2048]{1,0:T(8,128)(2,1)} %reduce-scatter.2.cloned.1.call-done) | copy-start | bytes 786436
Sparse Core Ops, SparseCore 0:
  22.4 50.0 all-gather.3
  80.1 74.2 reduce-scatter.1
